TPU v7x, 512 devices: a whole 4x8x8 slice. The times are simulated.
512 devices in a mesh: fsdp: 128 (over y, z, core), tensor: 4 (over x).
Axes of the slice: x: 4, y: 8, z: 8, core: 2. Of those that a mesh axis runs over, the one named last changes fastest.
Arguments:
- layer_inputs: bfloat16 [2, 49152, 5120], P(None, 'fsdp', 'tensor'), may hold values from -8 to 8, as said below
- out_grads: bfloat16 [2, 49152, 2560], P(None, 'fsdp', 'tensor'), may hold values from -8 to 8, as said below
- weight_grad: bfloat16 [2, 2560, 5120], P(None, 'fsdp', 'tensor'), may hold values from -0.059814453 to 0.059814453
- emb_grad: bfloat16 [50176, 2560], P('fsdp', 'tensor'), may hold values from -0.59765625 to 0.59765625
- counts: int32 [50176], P('fsdp'), may hold values from 0 to 250
- owner_pos: int32 [4, 30], P('tensor'), may hold values from 0 to 127, as said below
Outputs:
- update: bfloat16 [2, 2560, 5120], P(None, 'fsdp', 'tensor')
- owner_inverses: float32 [4, 128, 128, 128], P('tensor', 'fsdp')
- emb_update: bfloat16 [50176, 2560], P('fsdp', 'tensor')
Inputs may be any that keep to these rules, and one draw needn't show every extreme that they name: `layer_inputs`: every element lies within the stated range; inner units in groups of four share a common part. `out_grads`: every element lies within the stated range; features in groups of four share a common part. `owner_pos`: the 30 entries of a row are distinct; slot p belongs to fsdp index p; some fsdp index holds 1 block of each row.
All inputs are finite; a program needn't handle non-finite values. Where the computation divides by a largest or mean magnitude, that divisor is 1e-20 or more.
Results may differ from a plain program's by a relative error of at most 0.0062.
Values may be sent and summed in bfloat16 or wider, within the bound.
No kernel may reach another device: no remote copies, remote signals or barrier semaphores. Data moves between devices by JAX's collectives and lax.ppermute only.
A program may use at most 64 MiB of HBM per device.

v0:
```python
import jax
import jax.numpy as jnp
from jax import lax
from jax.sharding import PartitionSpec as P

BLK = 128
NS_ITERS = 8
DAMP = 0.02
EDAMP = 0.25


def newton_inverse(factor):
    identity = jnp.eye(factor.shape[-1], dtype=jnp.float32)
    damped = factor + DAMP * identity
    norm_scale = jnp.max(jnp.sum(jnp.abs(damped), axis=-1), axis=-1)
    approx = identity[None] / norm_scale[:, None, None]
    for sweep_idx in range(NS_ITERS):
        product = jnp.einsum("bij,bjk->bik", damped, approx, precision=lax.Precision.HIGHEST)
        approx = jnp.einsum(
            "bij,bjk->bik", approx, 2.0 * identity[None] - product, precision=lax.Precision.HIGHEST
        )
    return approx


def on_device(layer_inputs, out_grads, weight_grad, emb_grad, counts, owner_pos):
    fsdp_size = lax.axis_size("fsdp")
    layers, row_count, inner_local = layer_inputs.shape
    width_local = out_grads.shape[2]
    a_count = inner_local // BLK
    g_count = width_local // BLK
    input_blocks = layer_inputs.reshape(layers, row_count, a_count, BLK)
    a_part = jnp.einsum(
        "lrbi,lrbj->lbij", input_blocks, input_blocks, preferred_element_type=jnp.float32
    )
    grad_blocks = out_grads.reshape(layers, row_count, g_count, BLK)
    g_part = jnp.einsum(
        "lrbi,lrbj->lbij", grad_blocks, grad_blocks, preferred_element_type=jnp.float32
    )
    partials = jnp.concatenate([a_part, g_part], axis=1)
    count_part = jnp.sum(counts.astype(jnp.float32))
    block_total = layers * (a_count + g_count)
    own_table = owner_pos[0]
    slot_count = (block_total + fsdp_size - 1) // fsdp_size
    wanted = lax.axis_index("fsdp") * slot_count + jnp.arange(slot_count, dtype=jnp.int32)
    one_hot = (own_table[None, :] == wanted[:, None]).astype(jnp.float32)
    divisor = row_count * fsdp_size
    summed, count_total = lax.psum((partials, count_part), "fsdp")
    factors = (summed / divisor).reshape(-1, BLK, BLK)
    mine_blocks = jnp.einsum("sk,kij->sij", one_hot, factors, precision=lax.Precision.HIGHEST)
    held_inv = newton_inverse(mine_blocks) * jnp.max(one_hot, axis=1)[:, None, None]
    owner_out = held_inv[None]
    shared = lax.all_gather(held_inv.astype(jnp.bfloat16), "fsdp", axis=0, tiled=True)
    low_inv = jnp.take(shared, own_table, axis=0)
    low_inv = low_inv.reshape(layers, a_count + g_count, BLK, BLK)
    a_low = low_inv[:, :a_count]
    g_own = low_inv[:, a_count:]
    g_all = lax.all_gather(g_own, "tensor", axis=1, tiled=True)
    d_local = weight_grad.shape[1]
    grad_split = weight_grad.reshape(layers, d_local, a_count, BLK)
    right_done = jnp.einsum(
        "ldbi,lbij->ldbj", grad_split, a_low, preferred_element_type=jnp.float32
    )
    right_done = right_done.reshape(layers, d_local, inner_local).astype(jnp.bfloat16)
    columns = lax.all_to_all(right_done, "fsdp", split_axis=2, concat_axis=1, tiled=True)
    full_width = columns.shape[1]
    column_blocks = columns.reshape(layers, full_width // BLK, BLK, columns.shape[2])
    left_done = jnp.einsum(
        "lbij,lbjc->lbic", g_all, column_blocks, preferred_element_type=jnp.float32
    )
    left_done = left_done.reshape(columns.shape).astype(jnp.bfloat16)
    update = lax.all_to_all(left_done, "fsdp", split_axis=1, concat_axis=2, tiled=True)
    vocab_total = counts.shape[0] * fsdp_size
    frequency = counts.astype(jnp.float32) * vocab_total / count_total
    emb_update = (emb_grad.astype(jnp.float32) / (frequency + EDAMP)[:, None]).astype(jnp.bfloat16)
    return (update, owner_out, emb_update)


def solution(mesh):
    placed = (
        P(None, "fsdp", "tensor"),
        P(None, "fsdp", "tensor"),
        P(None, "fsdp", "tensor"),
        P("fsdp", "tensor"),
        P("fsdp"),
        P("tensor", None),
    )
    return jax.shard_map(
        on_device,
        mesh=mesh,
        in_specs=placed,
        out_specs=(P(None, "fsdp", "tensor"), P("tensor", "fsdp", None, None), P("fsdp", "tensor")),
        check_vma=False,
    )
```

profile of v0, /device:TPU:1, one launch (start us, length us, event | category | flops | bytes accessed | tf_op | source)
XLA Modules:
  0.0 627.3 jit_solution(3849056643370400006)
XLA Ops:
  7.2 0.0 all-reduce.2.cloned.1.call-start
  7.2 2.8 copy.41
  10.1 0.9 fusion.20
  11.0 1.6 copy.43
  12.6 0.5 fusion.21
  13.1 1.4 pad_maximum_fusion
  14.6 0.0 all-reduce.2.cloned.1.call-update
  14.6 0.0 all-gather.6.cloned.1.call-start
  14.6 0.6 copy-done.3
  15.2 0.6 fusion.14
  15.8 206.1 %all-reduce.2.cloned.1.call-done = f32[2,15,128,128]{3,2,1,0:T(8,128)} async-done(((f32[2,15,128,128]{3,2,1,0:T(8,128)}), f32[2,15,128,128]{3,2,1,0:T(8,128)}) %all-reduce.2.cloned.1.call-update) | async-done | bytes 1966096 | tf_op jit(solution)/shard_map/psum | solution.py:47
  221.9 1.7 broadcast_multiply_fusion
  223.6 1.9 fusion
  225.5 0.1 abs_reduce_fusion
  225.6 0.6 reduce_max.18
  226.9 0.2 convolution_subtract_fusion.7
  227.1 0.2 fusion.5
  227.3 0.2 convolution_subtract_fusion.6
  227.6 0.2 fusion.22
  227.8 0.2 convolution_subtract_fusion.5
  228.0 0.2 fusion.23
  228.2 0.2 convolution_subtract_fusion.4
  228.4 0.2 fusion.24
  228.6 0.2 convolution_subtract_fusion.3
  228.8 0.2 fusion.25
  229.0 0.2 convolution_subtract_fusion.2
  229.2 0.2 fusion.26
  229.5 0.2 convolution_subtract_fusion.1
  229.7 0.2 fusion.27
  229.9 0.2 convolution_subtract_fusion
  230.1 1.5 fusion.19
  231.6 0.0 all-gather.6.cloned.1.call-update
  231.6 0.0 all-gather.4.cloned.1.call-start
  231.7 0.5 broadcast.106
  232.2 0.7 reduce.8
  232.8 0.1 squeeze.5
  232.9 81.3 %all-gather.6.cloned.1.call-done = bf16[16384,128]{1,0:T(8,128)(2,1)} async-done(((bf16[128,128]{1,0:T(8,128)(2,1)}), bf16[16384,128]{1,0:T(8,128)(2,1)}) %all-gather.6.cloned.1.call-update) | async-done | bytes 4194320 | tf_op jit(solution)/shard_map/all_gather | solution.py:52
  314.3 2.9 gather_fusion
  317.2 0.2 broadcast_select_fusion
  317.4 0.7 slice.10
  318.1 0.0 all-gather.4.cloned.1.call-update
  318.2 0.6 convert_reduce_fusion
  318.8 247.1 %psum.15 = f32[]{:T(128)} all-reduce(f32[]{:T(128)} %convert_reduce_fusion), channel_id=1, replica_groups=mesh['fsdp'=128,'tensor'=4] {'fsdp'}, use_global_device_ids=true, to_apply=%region_5.0 | all-reduce | flops 1 | bytes 8 | tf_op jit(solution)/shard_map/psum | solution.py:47
  565.8 0.1 reshape.182
  565.9 0.3 fusion.2
  566.2 0.5 copy.59
  566.7 1.2 reshape.204
  567.9 10.2 %all-to-all-start = ((bf16[128,2,200]{2,1,0:T(2,128)(2,1)}), bf16[128,2,200]{2,1,0:T(2,128)(2,1)S(1)}, u32[]{:S(2)}, u32[]{:S(2)}) async-start(bf16[128,2,200]{2,1,0:T(2,128)(2,1)} %reshape.204), calls=%async_computation | async-start | bytes 262144 | tf_op jit(solution)/shard_map/all_to_all | solution.py:64
  578.1 0.7 divide_add_fusion
  578.7 11.6 %all-to-all-done = bf16[128,2,200]{2,1,0:T(2,128)(2,1)S(1)} async-done(((bf16[128,2,200]{2,1,0:T(2,128)(2,1)}), bf16[128,2,200]{2,1,0:T(2,128)(2,1)S(1)}, u32[]{:S(2)}, u32[]{:S(2)}) %all-to-all-start) | async-done | bytes 102432 | tf_op jit(solution)/shard_map/all_to_all | solution.py:64
  590.3 0.6 reshape.205
  590.9 0.1 copy.48
  591.1 1.4 reshape.183
  592.4 0.0 all-gather.4.cloned.1.call-done
  592.5 2.1 convolution_convert_fusion
  594.5 1.1 copy.60
  595.6 1.6 reshape.206
  597.2 6.1 all-to-all-start.1
  603.4 1.0 divide_convert_fusion
  604.3 11.4 %all-to-all-done.1 = bf16[128,2,200]{2,1,0:T(2,128)(2,1)S(1)} async-done(((bf16[128,2,200]{2,1,0:T(2,128)(2,1)}), bf16[128,2,200]{2,1,0:T(2,128)(2,1)S(1)}, u32[]{:S(2)}, u32[]{:S(2)}) %all-to-all-start.1) | async-done | bytes 102432 | tf_op jit(solution)/shard_map/all_to_all | solution.py:71
  615.7 1.0 reshape.207
  616.7 2.3 copy.61
  619.0 0.7 copy.53
  619.7 1.1 copy.54
  (10 shorter events, 0.0 us)
Async XLA Ops:
  7.2 214.7 %all-reduce.2.cloned.1.call-start = ((), (), s32[]{:S(2)}) async-start(), calls=%async_computation.2 | async-start | bytes 3932160 | tf_op jit(solution)/shard_map/psum | solution.py:47
  14.6 0.7 copy-start.3
  14.6 299.7 %all-gather.6.cloned.1.call-start = ((), (), s32[]{:S(2)}) async-start(), calls=%async_computation.4 | async-start | bytes 4227072 | tf_op jit(solution)/shard_map/all_gather | solution.py:52
  231.6 360.8 %all-gather.4.cloned.1.call-start = ((), (), s32[]{:S(2)}) async-start(), calls=%async_computation.3 | async-start | bytes 1638400 | tf_op jit(solution)/shard_map/all_gather | solution.py:57
  317.2 1.0 copy-start.2
  317.2 248.6 %copy-start.1 = (bf16[2,20,1280]{2,0,1:T(2,128)(2,1)S(1)}, bf16[2,20,1280]{2,0,1:T(2,128)(2,1)}, u32[]{:S(2)}) copy-start(bf16[2,20,1280]{2,0,1:T(2,128)(2,1)} %param.8) | copy-start | bytes 307204
  567.9 22.4 %all-to-all-start = ((bf16[128,2,200]{2,1,0:T(2,128)(2,1)}), bf16[128,2,200]{2,1,0:T(2,128)(2,1)S(1)}, u32[]{:S(2)}, u32[]{:S(2)}) async-start(bf16[128,2,200]{2,1,0:T(2,128)(2,1)} %reshape.204), calls=%async_computation | async-start | bytes 262144 | tf_op jit(solution)/shard_map/all_to_all | solution.py:64
  594.5 8.8 %copy-start = (bf16[392,640]{1,0:T(8,128)(2,1)S(1)}, bf16[392,640]{1,0:T(8,128)(2,1)}, u32[]{:S(2)}) copy-start(bf16[392,640]{1,0:T(8,128)(2,1)} %param.9) | copy-start | bytes 1505284
  597.2 18.5 %all-to-all-start.1 = ((bf16[128,2,200]{2,1,0:T(2,128)(2,1)}), bf16[128,2,200]{2,1,0:T(2,128)(2,1)S(1)}, u32[]{:S(2)}, u32[]{:S(2)}) async-start(bf16[128,2,200]{2,1,0:T(2,128)(2,1)} %reshape.206), calls=%async_computation.1 | async-start | bytes 262144 | tf_op jit(solution)/shard_map/all_to_all | solution.py:71
Sparse Core Ops, SparseCore 0:
  14.7 207.1 all-reduce.1
  231.7 82.4 all-gather.5
  318.3 25.3 all-gather.3
where the time goes:
time: 628 us; the launch traced here: 627 us
  waiting for transfers between devices  310 us (49%)
  blocking collectives  247 us (39%)
  local copies, waits for them, and re-layouts  20.9 us (3%)
  starting transfers between devices  16.4 us (3%)
  between operations  14.8 us (2%)
  matrix products  10.3 us (2%)
  other arithmetic  7.5 us (1%)
    psum x1, blocking collectives, on_device(): summed, count_total = lax.psum((partials, count_part), 'fsdp')  247 us
    psum x1, waiting for transfers between devices, on_device(): summed, count_total = lax.psum((partials, count_part), 'fsdp')  206 us
    all_gather x1, waiting for transfers between devices, on_device(): lax.all_gather(held_inv.astype(jnp.bfloat16), 'fsdp', axis=0, tiled=True)  81.3 us
  transfers between devices with their start and end apart: 5, of which 4 were waited for; matrix products, arithmetic and copies ran while one was open for 1% of the time, Pallas kernels for 0%

commit v1 on v0

--- a/solution.py
+++ b/solution.py
@@ -61,7 +61,12 @@
         "ldbi,lbij->ldbj", grad_split, a_low, preferred_element_type=jnp.float32
     )
     right_done = right_done.reshape(layers, d_local, inner_local).astype(jnp.bfloat16)
-    columns = lax.all_to_all(right_done, "fsdp", split_axis=2, concat_axis=1, tiled=True)
+    columns = jnp.concatenate(
+        lax.all_to_all(
+            jnp.stack(jnp.split(right_done, lax.axis_size("fsdp"), axis=2)), "fsdp", 0, 0
+        ),
+        axis=1,
+    )
     full_width = columns.shape[1]
     column_blocks = columns.reshape(layers, full_width // BLK, BLK, columns.shape[2])
     left_done = jnp.einsum(

time: 628 us -> 571 us (0.909)
  waiting for transfers between devices: 310 us -> 229 us
  local copies, waits for them, and re-layouts: 20.9 us -> 37.3 us
  starting transfers between devices: 16.4 us -> 23.3 us
    all_gather x1, waiting for transfers between devices: 81.3 us -> 0.02 us  [on_device(): lax.all_gather(held_inv.astype(jnp.bfloat16), 'fsdp', axis=0, tiled=True)]
    unnamed x16 -> x143, local copies, waits for them, and re-layouts: 11 us -> 22.3 us
    another operation x0 -> x3, local copies, waits for them, and re-layouts: none -> 6.48 us  [the longest x2 5.13 us: on_device(): jnp.stack(jnp.split(right_done, lax.axis_size('fsdp'), axis=2))]
  transfers between devices with their start and end apart: 5 -> 5, of which waited for: 4 -> 3; matrix products, arithmetic and copies ran while one was open for 1% -> 2% of each run, Pallas kernels for 0% -> 0%
where the time goes in v1:
time: 571 us; the launch traced here: 570 us
  blocking collectives  248 us (43%)
  waiting for transfers between devices  229 us (40%)
  local copies, waits for them, and re-layouts  37.3 us (7%)
  starting transfers between devices  23.3 us (4%)
  between operations  15 us (3%)
  matrix products  10.3 us (2%)
  other arithmetic  7.53 us (1%)
    psum x1, blocking collectives, on_device(): summed, count_total = lax.psum((partials, count_part), 'fsdp')  248 us
    psum x1, waiting for transfers between devices, on_device(): summed, count_total = lax.psum((partials, count_part), 'fsdp')  206 us
    unnamed x143, local copies, waits for them, and re-layouts  22.3 us
    all_to_all x1, starting transfers between devices, on_device(): lax.all_to_all(jnp.stack(jnp.split(right_done, lax.axis_size('fsdp'), axi...  13.1 us
    all_to_all x1, waiting for transfers between devices, on_device(): lax.all_to_all(jnp.stack(jnp.split(right_done, lax.axis_size('fsdp'), axi...  11.6 us
  transfers between devices with their start and end apart: 5, of which 3 were waited for; matrix products, arithmetic and copies ran while one was open for 2% of the time, Pallas kernels for 0%

profile of v1, /device:TPU:1, one launch (start us, length us, event | category | flops | bytes accessed | tf_op | source)
XLA Modules:
  0.0 570.1 jit_solution(7782323773077567545)
XLA Ops:
  7.2 2.8 copy.309
  10.1 0.9 fusion.20
  11.0 1.6 copy.311
  12.6 0.5 fusion.21
  13.1 1.5 pad_maximum_fusion
  14.7 0.6 copy-done.3
  15.3 0.6 fusion.14
  15.9 206.1 %all-reduce.2.cloned.1.call-done = f32[2,15,128,128]{3,2,1,0:T(8,128)} async-done(((f32[2,15,128,128]{3,2,1,0:T(8,128)}), f32[2,15,128,128]{3,2,1,0:T(8,128)}) %all-reduce.2.cloned.1.call-update) | async-done | bytes 1966096 | tf_op jit(solution)/shard_map/psum | solution.py:47
  221.9 1.7 broadcast_multiply_fusion
  223.7 1.9 fusion
  225.6 0.1 abs_reduce_fusion
  225.7 0.6 reduce_max.18
  227.0 0.2 convolution_subtract_fusion.7
  227.2 0.2 fusion.5
  227.4 0.2 convolution_subtract_fusion.6
  227.6 0.2 fusion.22
  227.8 0.2 convolution_subtract_fusion.5
  228.1 0.2 fusion.23
  228.3 0.2 convolution_subtract_fusion.4
  228.5 0.2 fusion.24
  228.7 0.2 convolution_subtract_fusion.3
  228.9 0.2 fusion.25
  229.1 0.2 convolution_subtract_fusion.2
  229.3 0.2 fusion.26
  229.5 0.2 convolution_subtract_fusion.1
  229.7 0.2 fusion.27
  230.0 0.2 convolution_subtract_fusion
  230.2 1.5 fusion.19
  231.7 0.6 convert_reduce_fusion
  232.3 247.7 %psum.15 = f32[]{:T(128)} all-reduce(f32[]{:T(128)} %convert_reduce_fusion), channel_id=1, replica_groups=mesh['fsdp'=128,'tensor'=4] {'fsdp'}, use_global_device_ids=true, to_apply=%region_5.0 | all-reduce | flops 1 | bytes 8 | tf_op jit(solution)/shard_map/psum | solution.py:47
  480.0 0.5 broadcast.106
  480.5 0.7 reduce.8
  481.4 2.9 gather_fusion
  484.3 0.2 broadcast_select_fusion
  484.5 0.7 slice.10
  485.3 0.3 fusion.2
  485.7 0.1 constant_dynamic-update-slice_fusion.126
  486.7 0.1 constant_dynamic-update-slice_fusion.115
  487.9 0.1 constant_dynamic-update-slice_fusion.102
  489.0 0.1 constant_dynamic-update-slice_fusion.89
  490.2 0.1 constant_dynamic-update-slice_fusion.76
  492.5 0.1 constant_dynamic-update-slice_fusion.51
  493.6 0.1 constant_dynamic-update-slice_fusion.38
  494.8 0.1 constant_dynamic-update-slice_fusion.25
  496.0 0.1 constant_dynamic-update-slice_fusion.12
  497.2 5.0 copy.315
  502.3 1.2 reshape.203
  503.5 13.1 %all-to-all-start = ((bf16[128,2,200]{2,1,0:T(2,128)(2,1)}), bf16[128,2,200]{2,1,0:T(2,128)(2,1)S(1)}, u32[]{:S(2)}, u32[]{:S(2)}) async-start(bf16[128,2,200]{2,1,0:T(2,128)(2,1)} %reshape.203), calls=%async_computation | async-start | bytes 262144 | tf_op jit(solution)/shard_map/all_to_all | solution.py:65
  516.6 0.6 divide_add_fusion
  517.2 11.6 %all-to-all-done = bf16[128,2,200]{2,1,0:T(2,128)(2,1)S(1)} async-done(((bf16[128,2,200]{2,1,0:T(2,128)(2,1)}), bf16[128,2,200]{2,1,0:T(2,128)(2,1)S(1)}, u32[]{:S(2)}, u32[]{:S(2)}) %all-to-all-start) | async-done | bytes 102432 | tf_op jit(solution)/shard_map/all_to_all | solution.py:65
  528.8 0.6 reshape.204
  529.5 0.5 bitcast_bitcast_fusion
  529.9 0.1 copy.316
  530.0 1.3 reshape_reshape.3
  531.4 2.1 convolution_convert_fusion
  533.5 1.1 copy.327
  534.6 1.6 reshape.205
  536.2 10.1 %all-to-all-start.1 = ((bf16[128,2,200]{2,1,0:T(2,128)(2,1)}), bf16[128,2,200]{2,1,0:T(2,128)(2,1)S(1)}, u32[]{:S(2)}, u32[]{:S(2)}) async-start(bf16[128,2,200]{2,1,0:T(2,128)(2,1)} %reshape.205), calls=%async_computation.1 | async-start | bytes 262144 | tf_op jit(solution)/shard_map/all_to_all | solution.py:76
  546.3 1.0 divide_convert_fusion
  547.2 11.3 %all-to-all-done.1 = bf16[128,2,200]{2,1,0:T(2,128)(2,1)S(1)} async-done(((bf16[128,2,200]{2,1,0:T(2,128)(2,1)}), bf16[128,2,200]{2,1,0:T(2,128)(2,1)S(1)}, u32[]{:S(2)}, u32[]{:S(2)}) %all-to-all-start.1) | async-done | bytes 102432 | tf_op jit(solution)/shard_map/all_to_all | solution.py:76
  558.5 1.0 reshape.206
  559.5 2.3 copy.328
  561.8 0.7 copy.321
  562.5 1.1 copy.322
  (141 shorter events, 11.0 us)
Async XLA Ops:
  7.2 214.8 %all-reduce.2.cloned.1.call-start = ((), (), s32[]{:S(2)}) async-start(), calls=%async_computation.2 | async-start | bytes 3932160 | tf_op jit(solution)/shard_map/psum | solution.py:47
  14.6 0.7 copy-start.3
  14.6 466.8 %all-gather.6.cloned.1.call-start = ((), (), s32[]{:S(2)}) async-start(), calls=%async_computation.4 | async-start | bytes 4227072 | tf_op jit(solution)/shard_map/all_gather | solution.py:52
  227.6 4.1 copy-start.2
  227.6 253.7 %copy-start.1 = (bf16[2,20,1280]{2,0,1:T(2,128)(2,1)S(1)}, bf16[2,20,1280]{2,0,1:T(2,128)(2,1)}, u32[]{:S(2)}) copy-start(bf16[2,20,1280]{2,0,1:T(2,128)(2,1)} %param.8) | copy-start | bytes 307204
  231.7 299.7 %all-gather.4.cloned.1.call-start = ((), (), s32[]{:S(2)}) async-start(), calls=%async_computation.3 | async-start | bytes 1638400 | tf_op jit(solution)/shard_map/all_gather | solution.py:57
  503.5 25.4 %all-to-all-start = ((bf16[128,2,200]{2,1,0:T(2,128)(2,1)}), bf16[128,2,200]{2,1,0:T(2,128)(2,1)S(1)}, u32[]{:S(2)}, u32[]{:S(2)}) async-start(bf16[128,2,200]{2,1,0:T(2,128)(2,1)} %reshape.203), calls=%async_computation | async-start | bytes 262144 | tf_op jit(solution)/shard_map/all_to_all | solution.py:65
  533.5 12.8 %copy-start = (bf16[392,640]{1,0:T(8,128)(2,1)S(1)}, bf16[392,640]{1,0:T(8,128)(2,1)}, u32[]{:S(2)}) copy-start(bf16[392,640]{1,0:T(8,128)(2,1)} %param.9) | copy-start | bytes 1505284
  536.2 22.3 %all-to-all-start.1 = ((bf16[128,2,200]{2,1,0:T(2,128)(2,1)}), bf16[128,2,200]{2,1,0:T(2,128)(2,1)S(1)}, u32[]{:S(2)}, u32[]{:S(2)}) async-start(bf16[128,2,200]{2,1,0:T(2,128)(2,1)} %reshape.205), calls=%async_computation.1 | async-start | bytes 262144 | tf_op jit(solution)/shard_map/all_to_all | solution.py:76
Sparse Core Ops, SparseCore 0:
  14.8 207.1 all-reduce.1
  231.8 82.5 all-gather.5
  496.7 29.1 all-gather.3
